TPU v7x, 256 devices: a whole 4x4x8 slice. The times are simulated.
256 devices in a mesh: req: 64 (over z, y, core), tp: 4 (over x).
Axes of the slice: x: 4, y: 4, z: 8, core: 2. Of those that a mesh axis runs over, the one named last changes fastest.
Arguments:
- hidden_in: bfloat16 [8192, 2048], P('req'), may hold values from -6 to 6
- attn_gain: float32 [2048], replicated, may hold values from 0.1 to 1.9
- w_query: bfloat16 [2048, 3072], P(None, 'tp'), may hold values from -0.125 to 0.125
- w_latent: bfloat16 [2048, 576], P(None, 'tp'), may hold values from -0.125 to 0.125
- kv_gain: float32 [512], replicated, may hold values from 0.1 to 1.9
- w_key_up: bfloat16 [512, 2048], P(None, 'tp'), may hold values from -0.25 to 0.25
- w_value_up: bfloat16 [512, 2048], P(None, 'tp'), may hold values from -0.25 to 0.25
- w_out: bfloat16 [2048, 2048], P('tp'), may hold values from -0.125 to 0.125
- moe_gain: float32 [2048], replicated, may hold values from 0.1 to 1.9
- w_gate: bfloat16 [64, 2048, 1408], P('req', None, 'tp'), may hold values from -0.125 to 0.125
- w_up: bfloat16 [64, 2048, 1408], P('req', None, 'tp'), may hold values from -0.125 to 0.125
- w_down: bfloat16 [64, 1408, 2048], P('req', 'tp'), may hold values from -0.15625 to 0.15625
- latent_cache: bfloat16 [2048, 64, 576], P('req'), may hold values from -3000 to 3000
- page_table: int32 [256, 8], P('req'), may hold values from 0 to 7, as said below
- cache_len: int32 [256], P('req'), may hold values from 1 to 512, 65536 in all
- parents: int32 [256, 3, 8], P('req'), may hold values from 0 to 7
- routes: int32 [8192, 6], P('req'), may hold values from 0 to 63, all different within a row; in each aligned block of 128 rows (0 to 127, 128 to 255, ...) at most 24 rows name the same one
- route_weights: float32 [8192, 6], P('req'), may hold values from 0.1 to 1
Outputs:
- layer_out: bfloat16 [8192, 2048], P('req', 'tp')
Inputs may be any that keep to these rules, and one draw needn't show every extreme that they name: `page_table`: each request's row lists the 8 pages of that request's block of the pool, each once. `routes`: each row names 6 different experts; in the rows of one index of req no expert is named more than 24 times, a bound that some block reaches.
All inputs are finite; a program needn't handle non-finite values. No bound on the sum of `cache_len` on one device may be relied on, other than what follows from the above.
Results may differ from a plain program's by a relative error of at most 0.015.
The roundings to bfloat16 on the way count: a program that leaves them out, or rounds other values in their place, can miss the bound.
Values may be sent and summed in bfloat16 or wider, within the bound.
No kernel may reach another device: no remote copies, remote signals or barrier semaphores. Data moves between devices by JAX's collectives and lax.ppermute only.
A program may use at most 128 MiB of HBM per device.

v0:
```python
import jax
import jax.numpy as jnp
from jax import lax
from jax.sharding import PartitionSpec as P

D = 2048
NOPE = 128
ROPE = 64
VDIM = 128
LATENT = 512
TOPK = 6
EXP_DEV = 1
BEAMS = 8
STEPS = 4
PAGE = 64
PAGES = 8
eps = 1e-06
rope_base = 50000.0


def rms_scale(values):
    return lax.rsqrt(jnp.mean(values * values, axis=-1, keepdims=True) + eps)


def rotate(values, cos_val, sin_val):
    half_rope = values.shape[-1] // 2
    first = values[..., :half_rope]
    second = values[..., half_rope:]
    return jnp.concatenate(
        [first * cos_val - second * sin_val, second * cos_val + first * sin_val], axis=-1
    )


def expert_math(arrived, gate_w, up_w, down_w):
    gate_val = jnp.einsum("nesd,edf->nesf", arrived, gate_w, preferred_element_type=jnp.float32)
    up_val = jnp.einsum("nesd,edf->nesf", arrived, up_w, preferred_element_type=jnp.float32)
    active = (jax.nn.silu(gate_val) * up_val).astype(jnp.bfloat16)
    return jnp.einsum("nesf,efd->nesd", active, down_w, preferred_element_type=jnp.float32)


def send_home(shares):
    return lax.all_to_all(shares, "req", split_axis=0, concat_axis=0, tiled=True)


def local(
    hidden_in,
    attn_gain,
    w_query,
    w_latent,
    kv_gain,
    w_key_up,
    w_value_up,
    w_out,
    moe_gain,
    w_gate,
    w_up,
    w_down,
    latent_cache,
    page_table,
    cache_len,
    parents,
    routes,
    route_weights,
):
    highest = lax.Precision.HIGHEST
    row_count = hidden_in.shape[0]
    req_local = cache_len.shape[0]
    heads_local = w_value_up.shape[1] // VDIM
    tp_count = lax.axis_size("tp")
    req_count = lax.axis_size("req")
    col_share = D // tp_count
    max_len = PAGES * PAGE
    hidden_f = hidden_in.astype(jnp.float32)
    normed = (hidden_f * rms_scale(hidden_f) * attn_gain).astype(jnp.bfloat16)
    positions = (
        cache_len.astype(jnp.float32)[:, None, None]
        + jnp.arange(STEPS, dtype=jnp.float32)[None, :, None]
        + jnp.zeros((1, 1, BEAMS), jnp.float32)
    ).reshape(row_count)
    frequency = rope_base ** (-2.0 * jnp.arange(ROPE // 2, dtype=jnp.float32) / ROPE)
    angles = positions[:, None] * frequency[None, :]
    cos_val = jnp.cos(angles)
    sin_val = jnp.sin(angles)
    queries = jnp.dot(normed, w_query, preferred_element_type=jnp.float32).reshape(
        row_count, heads_local, NOPE + ROPE
    )
    q_nope = queries[:, :, :NOPE].astype(jnp.bfloat16)
    q_rope = rotate(queries[:, :, NOPE:], cos_val[:, None, :], sin_val[:, None, :]).astype(
        jnp.bfloat16
    )
    kv_part = jnp.dot(normed, w_latent, preferred_element_type=jnp.float32)
    kv_all = lax.all_gather(kv_part, "tp", axis=1, tiled=True)
    new_lat = kv_all[:, :LATENT] * rms_scale(kv_all[:, :LATENT]) * kv_gain
    new_rope = rotate(kv_all[:, LATENT:], cos_val, sin_val)
    new_keys = jnp.concatenate([new_lat, new_rope], axis=1).astype(jnp.bfloat16)
    key_up = w_key_up.reshape(LATENT, heads_local, NOPE)
    q_lat = jnp.einsum("nhc,lhc->nhl", q_nope, key_up, preferred_element_type=jnp.float32).astype(
        jnp.bfloat16
    )
    query_key = jnp.concatenate([q_lat, q_rope], axis=2)
    pool_index = (jnp.arange(req_local, dtype=jnp.int32) * PAGES)[:, None] + page_table
    cache_keys = jnp.take(latent_cache, pool_index.reshape(-1), axis=0).reshape(
        req_local, max_len, LATENT + ROPE
    )
    live_mask = jnp.arange(max_len, dtype=jnp.int32)[None, :] < cache_len[:, None]
    score_scale = (NOPE + ROPE) ** (-0.5)
    grouped = query_key.reshape(req_local, STEPS * BEAMS * heads_local, LATENT + ROPE)
    s_cache = (
        jnp.einsum("rqd,rld->rql", grouped, cache_keys, preferred_element_type=jnp.float32)
        * score_scale
    )
    s_cache = jnp.where(live_mask[:, None, :], s_cache, -jnp.inf).reshape(
        req_local, STEPS, BEAMS, heads_local, max_len
    )
    fresh = new_keys.reshape(req_local, STEPS, BEAMS, LATENT + ROPE).astype(jnp.float32)
    parent_hot = (parents[..., None] == jnp.arange(BEAMS, dtype=jnp.int32)).astype(jnp.float32)
    identity = jnp.broadcast_to(jnp.eye(BEAMS, dtype=jnp.float32), (req_local, BEAMS, BEAMS))
    tail_rows = []
    for step_index in range(STEPS):
        lineage = identity
        pieces = [None] * STEPS
        for earlier in range(step_index, -1, -1):
            pieces[earlier] = jnp.einsum(
                "rba,rad->rbd", lineage, fresh[:, earlier], precision=highest
            )
            if earlier > 0:
                lineage = jnp.einsum(
                    "rba,rac->rbc", lineage, parent_hot[:, earlier - 1], precision=highest
                )
        for later in range(step_index + 1, STEPS):
            pieces[later] = jnp.zeros_like(pieces[0])
        tail_rows.append(jnp.stack(pieces, axis=2))
    tail_keys = jnp.stack(tail_rows, axis=1).astype(jnp.bfloat16)
    queries_tail = query_key.reshape(req_local, STEPS, BEAMS, heads_local, LATENT + ROPE)
    s_tail = (
        jnp.einsum(
            "rsbhd,rsbjd->rsbhj", queries_tail, tail_keys, preferred_element_type=jnp.float32
        )
        * score_scale
    )
    causal = jnp.arange(STEPS)[None, :] <= jnp.arange(STEPS)[:, None]
    s_tail = jnp.where(causal[None, :, None, None, :], s_tail, -jnp.inf)
    top_score = jnp.maximum(jnp.max(s_cache, axis=-1), jnp.max(s_tail, axis=-1))
    e_cache = jnp.exp(s_cache - top_score[..., None])
    e_tail = jnp.exp(s_tail - top_score[..., None])
    total = jnp.sum(e_cache, axis=-1) + jnp.sum(e_tail, axis=-1)
    p_cache = (e_cache / total[..., None]).astype(jnp.bfloat16)
    p_tail = (e_tail / total[..., None]).astype(jnp.bfloat16)
    context = jnp.einsum(
        "rsbhl,rld->rsbhd", p_cache, cache_keys[..., :LATENT], preferred_element_type=jnp.float32
    )
    context = context + jnp.einsum(
        "rsbhj,rsbjd->rsbhd", p_tail, tail_keys[..., :LATENT], preferred_element_type=jnp.float32
    )
    context = context.astype(jnp.bfloat16).reshape(row_count, heads_local, LATENT)
    value_up = w_value_up.reshape(LATENT, heads_local, VDIM)
    head_out = (
        jnp.einsum("nhl,lhv->nhv", context, value_up, preferred_element_type=jnp.float32)
        .astype(jnp.bfloat16)
        .reshape(row_count, heads_local * VDIM)
    )
    attn_part = jnp.dot(head_out, w_out, preferred_element_type=jnp.float32)
    expert_count = EXP_DEV * req_count
    capacity = min(row_count, 2 * row_count * TOPK // expert_count)
    slot_count = expert_count * capacity
    picks = routes.reshape(-1)
    pick_hot = (picks[:, None] == jnp.arange(expert_count, dtype=jnp.int32)[None, :]).astype(
        jnp.int32
    )
    before = jnp.cumsum(pick_hot, axis=0) - pick_hot
    ranks = jnp.sum(before * pick_hot, axis=1)
    slot_of = picks * capacity + ranks
    slot_hot = (slot_of[:, None] == jnp.arange(slot_count, dtype=jnp.int32)[None, :]).reshape(
        row_count, TOPK, slot_count
    )
    gather_rows = jnp.sum(slot_hot.astype(jnp.int32), axis=1).astype(jnp.bfloat16)
    weight_rows = jnp.sum(jnp.where(slot_hot, route_weights[:, :, None], 0.0), axis=1)
    tp_index = lax.axis_index("tp")
    col_start = tp_index * col_share
    attn_full = lax.psum(attn_part, "tp")
    resid_full = hidden_f + attn_full
    moe_in = (resid_full * rms_scale(resid_full) * moe_gain).astype(jnp.bfloat16)
    placed = jnp.dot(gather_rows.T, moe_in, preferred_element_type=jnp.float32).astype(jnp.bfloat16)
    partial_out = expert_math(
        lax.all_to_all(
            placed.reshape(req_count, EXP_DEV, capacity, moe_in.shape[1]),
            "req",
            split_axis=0,
            concat_axis=0,
            tiled=True,
        ),
        w_gate,
        w_up,
        w_down,
    )
    shares = lax.psum_scatter(partial_out, "tp", scatter_dimension=3, tiled=True)
    returned = send_home(shares.astype(jnp.bfloat16))
    resid_cols = lax.dynamic_slice_in_dim(resid_full, col_start, col_share, 1)
    combined = jnp.dot(
        weight_rows, returned.reshape(slot_count, col_share).astype(jnp.float32), precision=highest
    )
    return (resid_cols + combined).astype(jnp.bfloat16)


def solution(mesh):
    in_specs = (
        P("req", None),
        P(),
        P(None, "tp"),
        P(None, "tp"),
        P(),
        P(None, "tp"),
        P(None, "tp"),
        P("tp", None),
        P(),
        P("req", None, "tp"),
        P("req", None, "tp"),
        P("req", "tp", None),
        P("req", None, None),
        P("req", None),
        P("req"),
        P("req", None, None),
        P("req", None),
        P("req", None),
    )
    out_specs = P("req", "tp")
    return jax.shard_map(local, mesh=mesh, in_specs=in_specs, out_specs=out_specs, check_vma=False)
```

profile of v0, /device:TPU:1, one launch (start us, length us, event | category | flops | bytes accessed | tf_op | source)
XLA Modules:
  0.0 477.5 jit_solution(17207747423116017685)
XLA Ops:
  6.5 0.6 multiply_power_fusion
  7.1 0.8 iota_compare_fusion.3
  8.2 1.2 fusion.40
  9.5 1.6 fusion.63
  11.1 11.2 %all_gather.3 = f32[128,576]{0,1:T(8,128)S(1)} all-gather(f32[128,144]{0,1:T(8,128)S(1)} %fusion.63), channel_id=1, replica_groups=mesh['req'=64,'tp'=4] {'tp'}, dimensions={1}, use_global_device_ids=true | all-gather | bytes 368640 | tf_op jit(solution)/shard_map/all_gather | solution.py:92
  22.4 0.8 multiply_convert_fusion.2
  23.2 1.6 copy.150
  25.1 0.8 multiply_cosine_fusion
  26.1 0.1 fusion.70
  26.3 0.1 fusion.72
  26.4 1.0 pad_maximum_fusion.2
  27.4 0.8 fusion.37
  28.3 0.8 fusion.34
  29.1 0.8 fusion.38
  30.1 0.8 fusion.30
  30.9 0.8 fusion.32
  31.6 0.8 fusion.35
  32.4 0.8 fusion.39
  33.2 0.5 iota_compare_fusion.6
  33.7 0.5 iota_multiply_fusion
  34.2 0.7 iota_compare_fusion.4
  35.0 0.8 fusion.36
  35.8 0.8 fusion.33
  36.6 0.8 fusion.31
  37.3 0.7 copy.144
  38.0 0.7 copy.146
  38.8 2.4 fusion.65
  41.5 1.4 fusion.22
  42.9 0.9 subtract_convert_fusion
  44.0 0.5 copy.147
  44.5 1.2 reshape.300
  46.0 4.1 gather_fusion
  50.1 2.1 bitcast_select_fusion
  52.3 2.0 fusion.86
  54.5 0.9 maximum_bitcast_fusion
  55.6 3.1 fusion.87
  58.9 0.2 copy.158
  59.0 1.2 fusion.58
  60.2 2.6 reshape.302
  62.8 1.5 exponential_reduce_fusion
  64.5 0.2 copy.160
  64.6 1.7 fusion.51
  66.3 0.9 fusion.21
  67.3 1.4 copy.179
  68.7 0.3 convolution_convert_fusion.2
  69.1 1.5 fusion.88
  70.6 0.2 reduce-scatter.2.cloned.1.call-start
  71.2 1.8 reduce-window.6
  73.0 0.3 slice_reduce_fusion
  73.3 0.1 fusion.61
  73.7 0.7 convert_reduce_fusion
  74.4 50.8 %all-reduce.2.cloned.1.call-done = f32[128,2048]{1,0:T(8,128)} async-done(((f32[128,2048]{1,0:T(8,128)}), f32[128,2048]{1,0:T(8,128)}) %all-reduce.2.cloned.1.call-update) | async-done | bytes 1048592 | tf_op jit(solution)/shard_map/psum | solution.py:180
  125.1 1.4 multiply_reduce_fusion
  126.6 1.9 convolution_convert_fusion
  128.5 151.6 %all_to_all.10 = bf16[64,1,24,2048]{3,2,1,0:T(8,128)(2,1)S(1)} all-to-all(bf16[64,1,24,2048]{3,2,1,0:T(8,128)(2,1)S(1)} %bitcast.216), channel_id=1, replica_groups=mesh['req'=64,'tp'=4] {'req'}, dimensions={0} | all-to-all | bytes 12582912 | tf_op jit(solution)/shard_map/all_to_all | solution.py:185
  280.1 2.6 copy-done.2
  282.6 5.0 %fusion.2 = f32[64,24,352]{2,1,0:T(8,128)} fusion(bf16[64,1,24,2048]{3,2,1,0:T(8,128)(2,1)S(1)} %all_to_all.10, bf16[1,2048,352]{1,2,0:T(8,128)(2,1)S(1)} %copy-done.25), kind=kOutput, calls=%fused_computation.4 | convolution fusion | flops 2214592512 | bytes 9895936 | tf_op jit(solution)/shard_map/nesd,edf->nesf/dot_general | solution.py:35
  287.7 12.3 %convolution_bitcast_fusion = f32[64,1,24,2048]{3,2,0,1:T(8,128)} fusion(bf16[1,352,2048]{2,1,0:T(8,128)(2,1)S(1)} %copy-done.26, bf16[1,2048,352]{1,2,0:T(8,128)(2,1)} %param.28, bf16[64,1,24,2048]{3,2,1,0:T(8,128)(2,1)} %copy-done.2, f32[64,24,352]{2,1,0:T(8,128)} %fusion.2), kind=kOutput, calls=%fused_computation.6 | convolution fusion | flops 4432429056 | bytes 23920640 | tf_op jit(solution)/shard_map/nesf,efd->nesd/dot_general | solution.py:38
  300.0 114.4 %reduce-scatter.2.cloned.1.call-done = f32[64,1,24,512]{3,2,0,1:T(8,128)} async-done(((f32[64,1,24,2048]{3,2,0,1:T(8,128)}), f32[64,1,24,512]{3,2,0,1:T(8,128)}) %reduce-scatter.2.cloned.1.call-update) | async-done | bytes 3145744 | tf_op jit(solution)/shard_map/reduce_scatter | solution.py:196
  414.4 3.2 convert_bitcast_fusion
  417.7 10.9 %all-to-all-start.1 = ((bf16[64,1,24,512]{3,2,1,0:T(8,128)(2,1)}), bf16[64,1,24,512]{3,2,1,0:T(8,128)(2,1)}, u32[]{:S(2)}, u32[]{:S(2)}) async-start(bf16[64,1,24,512]{3,2,1,0:T(8,128)(2,1)} %convert_bitcast_fusion), calls=%async_computation.2 | async-start | bytes 3145728 | tf_op jit(solution)/shard_map/all_to_all | solution.py:42
  428.6 1.5 select_reduce_fusion
  430.2 37.4 %all-to-all-done.1 = bf16[64,1,24,512]{3,2,1,0:T(8,128)(2,1)} async-done(((bf16[64,1,24,512]{3,2,1,0:T(8,128)(2,1)}), bf16[64,1,24,512]{3,2,1,0:T(8,128)(2,1)}, u32[]{:S(2)}, u32[]{:S(2)}) %all-to-all-start.1) | async-done | bytes 1572896 | tf_op jit(solution)/shard_map/all_to_all | solution.py:42
  467.6 3.1 fusion.29
  (104 shorter events, 3.2 us)
Async XLA Ops:
  6.5 32.2 %copy-start = (bf16[2048,768]{1,0:T(8,128)(2,1)S(1)}, bf16[2048,768]{1,0:T(8,128)(2,1)}, u32[]{:S(2)}) copy-start(bf16[2048,768]{1,0:T(8,128)(2,1)} %param.20) | copy-start | bytes 9437188
  6.5 15.8 %copy-start.21 = (f32[512]{0:T(512)S(1)}, f32[512]{0:T(512)}, u32[]{:S(2)}) copy-start(f32[512]{0:T(512)} %param.22) | copy-start | bytes 6148
  6.5 18.3 %copy-start.23 = (s32[4]{0:T(128)S(1)}, s32[4]{0:T(128)}, u32[]{:S(2)}) copy-start(s32[4]{0:T(128)} %param.32) | copy-start | bytes 52
  6.5 118.6 %all-reduce.2.cloned.1.call-start = ((), (), s32[]{:S(2)}) async-start(), calls=%async_computation.3 | async-start | bytes 2097152 | tf_op jit(solution)/shard_map/psum | solution.py:180
  9.5 29.3 %copy-start.18 = (f32[2048]{0:T(1024)S(1)}, f32[2048]{0:T(1024)}, u32[]{:S(2)}) copy-start(f32[2048]{0:T(1024)} %param.19) | copy-start | bytes 24580
  42.9 2.8 copy-start.22
  42.9 2.8 copy-start.24
  44.0 6.1 %copy-start.6 = (bf16[128,4,576]{2,0,1:T(8,128)(2,1)}, bf16[128,4,576]{2,0,1:T(8,128)(2,1)S(1)}, u32[]{:S(2)}) copy-start(bf16[128,4,576]{2,0,1:T(8,128)(2,1)S(1)} %pad_maximum_fusion) | copy-start | bytes 1769476
  50.1 2.1 copy-start.5
  52.2 2.3 copy-start.10
  52.2 2.3 copy-start.11
  52.2 2.3 copy-start.12
  52.2 2.3 copy-start.13
  52.2 2.3 copy-start.14
  52.2 2.3 copy-start.15
  52.3 2.3 copy-start.16
  54.3 1.4 copy-start.27
  55.6 3.1 copy-start.7
  58.7 5.9 %slice-start = ((bf16[4,4,8,4,576]{4,2,0,3,1:T(8,128)(2,1)}), bf16[4,4,8,4,512]{4,2,0,3,1:T(8,128)(2,1)S(1)}, s32[]{:S(2)}) async-start(bf16[4,4,8,4,576]{4,2,0,3,1:T(8,128)(2,1)} %copy-done.7), calls=%async_computation.5 | async-start | bytes 1048576 | tf_op jit(solution)/shard_map/slice | solution.py:153
  64.6 1.7 copy-start.9
  67.3 1.8 copy-start.8
  69.0 1.8 copy-start.17
  70.5 54.6 %copy-start.4 = (bf16[128,2048]{1,0:T(8,128)(2,1)S(1)}, bf16[128,2048]{1,0:T(8,128)(2,1)}, u32[]{:S(2)}) copy-start(bf16[128,2048]{1,0:T(8,128)(2,1)} %param.18) | copy-start | bytes 1572868
  70.6 343.9 %reduce-scatter.2.cloned.1.call-start = ((), (), s32[]{:S(2)}) async-start(), calls=%async_computation.4 | async-start | bytes 15728640 | tf_op jit(solution)/shard_map/reduce_scatter | solution.py:196
  70.9 55.7 %copy-start.19 = (f32[2048]{0:T(1024)S(1)}, f32[2048]{0:T(1024)}, u32[]{:S(2)}) copy-start(f32[2048]{0:T(1024)} %param.26) | copy-start | bytes 24580
  126.6 1.9 copy-start.3
  128.5 154.2 %copy-start.25 = (bf16[1,2048,352]{1,2,0:T(8,128)(2,1)S(1)}, bf16[1,2048,352]{1,2,0:T(8,128)(2,1)}, u32[]{:S(2)}) copy-start(bf16[1,2048,352]{1,2,0:T(8,128)(2,1)} %param.27) | copy-start | bytes 4325380
  280.1 2.6 copy-start.2
  282.6 5.0 %copy-start.26 = (bf16[1,352,2048]{2,1,0:T(8,128)(2,1)S(1)}, bf16[1,352,2048]{2,1,0:T(8,128)(2,1)}, u32[]{:S(2)}) copy-start(bf16[1,352,2048]{2,1,0:T(8,128)(2,1)} %param.29) | copy-start | bytes 4325380
  417.7 11.0 %copy-start.20 = (f32[128,6]{0,1:T(8,128)S(1)}, f32[128,6]{0,1:T(8,128)}, u32[]{:S(2)}) copy-start(f32[128,6]{0,1:T(8,128)} %param.35) | copy-start | bytes 9220
  417.7 49.9 %all-to-all-start.1 = ((bf16[64,1,24,512]{3,2,1,0:T(8,128)(2,1)}), bf16[64,1,24,512]{3,2,1,0:T(8,128)(2,1)}, u32[]{:S(2)}, u32[]{:S(2)}) async-start(bf16[64,1,24,512]{3,2,1,0:T(8,128)(2,1)} %convert_bitcast_fusion), calls=%async_computation.2 | async-start | bytes 3145728 | tf_op jit(solution)/shard_map/all_to_all | solution.py:42
  428.6 42.1 %copy-start.1 = (bf16[2048,768]{1,0:T(8,128)(2,1)S(1)}, bf16[2048,768]{1,0:T(8,128)(2,1)}, u32[]{:S(2)}) copy-start(bf16[2048,768]{1,0:T(8,128)(2,1)} %param.20) | copy-start | bytes 9437188
Sparse Core Ops, SparseCore 0:
  70.7 54.3 all-reduce.1
  300.1 114.2 reduce-scatter.1
where the time goes:
time: 478 us
  waiting for transfers between devices  203 us (42%)
  blocking collectives  163 us (34%)
  matrix products  45.9 us (10%)
  other arithmetic  23 us (5%)
  local copies, waits for them, and re-layouts  18.1 us (4%)
  between operations  14 us (3%)
  starting transfers between devices  11.2 us (2%)
    all_to_all x1, blocking collectives, local(): lax.all_to_all(placed.reshape(req_count, EXP_DEV, capacity, moe_in.shape[...  152 us
    reduce_scatter x1, waiting for transfers between devices, local(): lax.psum_scatter(partial_out, 'tp', scatter_dimension=3, tiled=True)  114 us
    psum x1, waiting for transfers between devices, local(): attn_full = lax.psum(attn_part, 'tp')  50.8 us
    all_to_all x1, waiting for transfers between devices, send_home(): lax.all_to_all(shares, 'req', split_axis=0, concat_axis=0, tiled=True)  37.4 us
    dot_general x1, matrix products, expert_math(): jnp.einsum('nesf,efd->nesd', active, down_w, preferred_element_type=jnp.f...  12.3 us
    all_gather x1, blocking collectives, local(): kv_all = lax.all_gather(kv_part, 'tp', axis=1, tiled=True)  11.2 us
    all_to_all x1, starting transfers between devices, send_home(): lax.all_to_all(shares, 'req', split_axis=0, concat_axis=0, tiled=True)  10.9 us
  transfers between devices with their start and end apart: 3, of which 3 were waited for; matrix products, arithmetic and copies ran while one was open for 1% of the time, Pallas kernels for 0%

commit v1 on v0

--- a/solution.py
+++ b/solution.py
@@ -177,7 +177,7 @@
     weight_rows = jnp.sum(jnp.where(slot_hot, route_weights[:, :, None], 0.0), axis=1)
     tp_index = lax.axis_index("tp")
     col_start = tp_index * col_share
-    attn_full = lax.psum(attn_part, "tp")
+    attn_full = jnp.sum(lax.all_gather(attn_part, "tp"), axis=0)
     resid_full = hidden_f + attn_full
     moe_in = (resid_full * rms_scale(resid_full) * moe_gain).astype(jnp.bfloat16)
     placed = jnp.dot(gather_rows.T, moe_in, preferred_element_type=jnp.float32).astype(jnp.bfloat16)

time: 478 us -> 481 us (level)
    all_gather x0 -> x1, waiting for transfers between devices: none -> 52 us  [local(): attn_full = jnp.sum(lax.all_gather(attn_part, 'tp'), axis=0)]
    psum x1 -> x0, waiting for transfers between devices: 50.8 us -> none  [local(): attn_full = lax.psum(attn_part, 'tp')]
where the time goes in v1:
time: 481 us; the launch traced here: 480 us
  waiting for transfers between devices  203 us (42%)
  blocking collectives  161 us (33%)
  matrix products  45.9 us (10%)
  other arithmetic  26.7 us (6%)
  local copies, waits for them, and re-layouts  18.1 us (4%)
  between operations  13.9 us (3%)
  starting transfers between devices  11.2 us (2%)
    all_to_all x1, blocking collectives, local(): lax.all_to_all(placed.reshape(req_count, EXP_DEV, capacity, moe_in.shape[...  150 us
    reduce_scatter x1, waiting for transfers between devices, local(): lax.psum_scatter(partial_out, 'tp', scatter_dimension=3, tiled=True)  114 us
    all_gather x1, waiting for transfers between devices, local(): attn_full = jnp.sum(lax.all_gather(attn_part, 'tp'), axis=0)  52 us
    all_to_all x1, waiting for transfers between devices, send_home(): lax.all_to_all(shares, 'req', split_axis=0, concat_axis=0, tiled=True)  37.4 us
    dot_general x1, matrix products, expert_math(): jnp.einsum('nesf,efd->nesd', active, down_w, preferred_element_type=jnp.f...  12.3 us
    all_gather x1, blocking collectives, local(): kv_all = lax.all_gather(kv_part, 'tp', axis=1, tiled=True)  11.2 us
    all_to_all x1, starting transfers between devices, send_home(): lax.all_to_all(shares, 'req', split_axis=0, concat_axis=0, tiled=True)  10.9 us
  transfers between devices with their start and end apart: 3, of which 3 were waited for; matrix products, arithmetic and copies ran while one was open for 1% of the time, Pallas kernels for 0%

profile of v1, /device:TPU:1, one launch (start us, length us, event | category | flops | bytes accessed | tf_op | source)
XLA Modules:
  0.0 480.4 jit_solution(8657390105484211253)
XLA Ops:
  6.5 0.6 multiply_power_fusion
  7.1 0.8 iota_compare_fusion.3
  8.2 1.2 fusion.40
  9.5 1.6 fusion.63
  11.1 11.2 %all_gather.9 = f32[128,576]{0,1:T(8,128)S(1)} all-gather(f32[128,144]{0,1:T(8,128)S(1)} %fusion.63), channel_id=1, replica_groups=mesh['req'=64,'tp'=4] {'tp'}, dimensions={1}, use_global_device_ids=true | all-gather | bytes 368640 | tf_op jit(solution)/shard_map/all_gather | solution.py:92
  22.4 0.8 multiply_convert_fusion.2
  23.2 1.6 copy.150
  25.1 0.8 multiply_cosine_fusion
  26.1 0.1 fusion.70
  26.3 0.1 fusion.72
  26.4 1.0 pad_maximum_fusion.2
  27.4 0.8 fusion.37
  28.3 0.8 fusion.34
  29.1 0.8 fusion.38
  30.1 0.8 fusion.30
  30.9 0.8 fusion.32
  31.6 0.8 fusion.35
  32.4 0.8 fusion.39
  33.2 0.5 iota_compare_fusion.6
  33.7 0.5 iota_multiply_fusion
  34.2 0.7 iota_compare_fusion.4
  35.0 0.8 fusion.36
  35.8 0.8 fusion.33
  36.6 0.8 fusion.31
  37.3 0.7 copy.144
  38.0 0.7 copy.146
  38.8 2.4 fusion.65
  41.5 1.4 fusion.22
  42.9 0.9 subtract_convert_fusion
  44.0 0.5 copy.147
  44.5 1.2 reshape.300
  46.0 4.1 gather_fusion
  50.1 2.1 bitcast_select_fusion
  52.3 2.0 fusion.86
  54.5 0.9 maximum_bitcast_fusion
  55.6 3.1 fusion.87
  58.9 0.2 copy.158
  59.0 1.2 fusion.58
  60.2 2.6 reshape.302
  62.8 1.5 exponential_reduce_fusion
  64.5 0.2 copy.160
  64.6 1.7 fusion.51
  66.3 0.9 fusion.21
  67.3 1.4 copy.179
  68.7 0.3 convolution_convert_fusion.2
  69.1 1.4 fusion.88
  70.5 0.2 reduce-scatter.2.cloned.1.call-start
  71.2 1.8 reduce-window.6
  73.0 0.3 slice_reduce_fusion
  73.6 0.7 convert_reduce_fusion
  74.3 52.0 %all-gather.3.cloned.1.call-done = f32[512,2048]{1,0:T(8,128)} async-done(((f32[128,2048]{1,0:T(8,128)}), f32[512,2048]{1,0:T(8,128)}) %all-gather.3.cloned.1.call-update) | async-done | bytes 4194320 | tf_op jit(solution)/shard_map/all_gather | solution.py:180
  126.3 3.6 reduce_sum.90
  129.9 1.5 multiply_reduce_fusion
  131.4 1.9 convolution_convert_fusion
  133.3 150.2 %all_to_all.10 = bf16[64,1,24,2048]{3,2,1,0:T(8,128)(2,1)S(1)} all-to-all(bf16[64,1,24,2048]{3,2,1,0:T(8,128)(2,1)S(1)} %bitcast.217), channel_id=1, replica_groups=mesh['req'=64,'tp'=4] {'req'}, dimensions={0} | all-to-all | bytes 12582912 | tf_op jit(solution)/shard_map/all_to_all | solution.py:185
  283.5 2.6 copy-done.2
  286.1 5.0 %fusion.2 = f32[64,24,352]{2,1,0:T(8,128)} fusion(bf16[64,1,24,2048]{3,2,1,0:T(8,128)(2,1)S(1)} %all_to_all.10, bf16[1,2048,352]{1,2,0:T(8,128)(2,1)S(1)} %copy-done.25), kind=kOutput, calls=%fused_computation.4 | convolution fusion | flops 2214592512 | bytes 9895936 | tf_op jit(solution)/shard_map/nesd,edf->nesf/dot_general | solution.py:35
  291.1 12.3 %convolution_bitcast_fusion = f32[64,1,24,2048]{3,2,0,1:T(8,128)} fusion(bf16[1,352,2048]{2,1,0:T(8,128)(2,1)S(1)} %copy-done.26, bf16[1,2048,352]{1,2,0:T(8,128)(2,1)} %param.28, bf16[64,1,24,2048]{3,2,1,0:T(8,128)(2,1)} %copy-done.2, f32[64,24,352]{2,1,0:T(8,128)} %fusion.2), kind=kOutput, calls=%fused_computation.6 | convolution fusion | flops 4432429056 | bytes 23920640 | tf_op jit(solution)/shard_map/nesf,efd->nesd/dot_general | solution.py:38
  303.4 113.9 %reduce-scatter.2.cloned.1.call-done = f32[64,1,24,512]{3,2,0,1:T(8,128)} async-done(((f32[64,1,24,2048]{3,2,0,1:T(8,128)}), f32[64,1,24,512]{3,2,0,1:T(8,128)}) %reduce-scatter.2.cloned.1.call-update) | async-done | bytes 3145744 | tf_op jit(solution)/shard_map/reduce_scatter | solution.py:196
  417.3 3.2 convert_bitcast_fusion
  420.6 10.9 %all-to-all-start.1 = ((bf16[64,1,24,512]{3,2,1,0:T(8,128)(2,1)}), bf16[64,1,24,512]{3,2,1,0:T(8,128)(2,1)}, u32[]{:S(2)}, u32[]{:S(2)}) async-start(bf16[64,1,24,512]{3,2,1,0:T(8,128)(2,1)} %convert_bitcast_fusion), calls=%async_computation.2 | async-start | bytes 3145728 | tf_op jit(solution)/shard_map/all_to_all | solution.py:42
  431.6 1.5 select_reduce_fusion
  433.1 37.4 %all-to-all-done.1 = bf16[64,1,24,512]{3,2,1,0:T(8,128)(2,1)} async-done(((bf16[64,1,24,512]{3,2,1,0:T(8,128)(2,1)}), bf16[64,1,24,512]{3,2,1,0:T(8,128)(2,1)}, u32[]{:S(2)}, u32[]{:S(2)}) %all-to-all-start.1) | async-done | bytes 1572896 | tf_op jit(solution)/shard_map/all_to_all | solution.py:42
  470.5 3.1 fusion.29
  (105 shorter events, 3.4 us)
Async XLA Ops:
  6.5 32.2 %copy-start = (bf16[2048,768]{1,0:T(8,128)(2,1)S(1)}, bf16[2048,768]{1,0:T(8,128)(2,1)}, u32[]{:S(2)}) copy-start(bf16[2048,768]{1,0:T(8,128)(2,1)} %param.20) | copy-start | bytes 9437188
  6.5 15.8 %copy-start.21 = (f32[512]{0:T(512)S(1)}, f32[512]{0:T(512)}, u32[]{:S(2)}) copy-start(f32[512]{0:T(512)} %param.22) | copy-start | bytes 6148
  6.5 18.3 %copy-start.23 = (s32[4]{0:T(128)S(1)}, s32[4]{0:T(128)}, u32[]{:S(2)}) copy-start(s32[4]{0:T(128)} %param.32) | copy-start | bytes 52
  6.5 119.7 %all-gather.3.cloned.1.call-start = ((), (), s32[]{:S(2)}) async-start(), calls=%async_computation.4 | async-start | bytes 5242880 | tf_op jit(solution)/shard_map/all_gather | solution.py:180
  9.5 29.3 %copy-start.18 = (f32[2048]{0:T(1024)S(1)}, f32[2048]{0:T(1024)}, u32[]{:S(2)}) copy-start(f32[2048]{0:T(1024)} %param.19) | copy-start | bytes 24580
  42.9 2.8 copy-start.22
  42.9 2.8 copy-start.24
  44.0 6.1 %copy-start.6 = (bf16[128,4,576]{2,0,1:T(8,128)(2,1)}, bf16[128,4,576]{2,0,1:T(8,128)(2,1)S(1)}, u32[]{:S(2)}) copy-start(bf16[128,4,576]{2,0,1:T(8,128)(2,1)S(1)} %pad_maximum_fusion) | copy-start | bytes 1769476
  50.1 2.1 copy-start.5
  52.2 2.3 copy-start.10
  52.2 2.3 copy-start.11
  52.2 2.3 copy-start.12
  52.2 2.3 copy-start.13
  52.2 2.3 copy-start.14
  52.2 2.3 copy-start.15
  52.3 2.3 copy-start.16
  54.3 1.4 copy-start.27
  55.6 3.1 copy-start.7
  58.7 5.9 %slice-start = ((bf16[4,4,8,4,576]{4,2,0,3,1:T(8,128)(2,1)}), bf16[4,4,8,4,512]{4,2,0,3,1:T(8,128)(2,1)S(1)}, s32[]{:S(2)}) async-start(bf16[4,4,8,4,576]{4,2,0,3,1:T(8,128)(2,1)} %copy-done.7), calls=%async_computation.5 | async-start | bytes 1048576 | tf_op jit(solution)/shard_map/slice | solution.py:153
  64.6 1.7 copy-start.9
  67.3 1.8 copy-start.8
  69.0 1.7 copy-start.17
  70.5 346.8 %reduce-scatter.2.cloned.1.call-start = ((), (), s32[]{:S(2)}) async-start(), calls=%async_computation.3 | async-start | bytes 15728640 | tf_op jit(solution)/shard_map/reduce_scatter | solution.py:196
  126.3 3.6 copy-start.4
  129.9 1.5 copy-start.19
  131.4 1.9 copy-start.3
  133.3 152.8 %copy-start.25 = (bf16[1,2048,352]{1,2,0:T(8,128)(2,1)S(1)}, bf16[1,2048,352]{1,2,0:T(8,128)(2,1)}, u32[]{:S(2)}) copy-start(bf16[1,2048,352]{1,2,0:T(8,128)(2,1)} %param.27) | copy-start | bytes 4325380
  283.5 2.6 copy-start.2
  286.1 5.0 %copy-start.26 = (bf16[1,352,2048]{2,1,0:T(8,128)(2,1)S(1)}, bf16[1,352,2048]{2,1,0:T(8,128)(2,1)}, u32[]{:S(2)}) copy-start(bf16[1,352,2048]{2,1,0:T(8,128)(2,1)} %param.29) | copy-start | bytes 4325380
  420.6 11.0 %copy-start.20 = (f32[128,6]{0,1:T(8,128)S(1)}, f32[128,6]{0,1:T(8,128)}, u32[]{:S(2)}) copy-start(f32[128,6]{0,1:T(8,128)} %param.35) | copy-start | bytes 9220
  420.6 49.9 %all-to-all-start.1 = ((bf16[64,1,24,512]{3,2,1,0:T(8,128)(2,1)}), bf16[64,1,24,512]{3,2,1,0:T(8,128)(2,1)}, u32[]{:S(2)}, u32[]{:S(2)}) async-start(bf16[64,1,24,512]{3,2,1,0:T(8,128)(2,1)} %convert_bitcast_fusion), calls=%async_computation.2 | async-start | bytes 3145728 | tf_op jit(solution)/shard_map/all_to_all | solution.py:42
  431.5 42.1 %copy-start.1 = (bf16[2048,768]{1,0:T(8,128)(2,1)S(1)}, bf16[2048,768]{1,0:T(8,128)(2,1)}, u32[]{:S(2)}) copy-start(bf16[2048,768]{1,0:T(8,128)(2,1)} %param.20) | copy-start | bytes 9437188
Sparse Core Ops, SparseCore 0:
  70.6 55.6 all-gather.2
  303.5 113.7 reduce-scatter.1
